TPU v7x, 256 devices: a whole 4x4x8 slice. The times are simulated.
256 devices in a mesh: dp: 8 (over x, core), expert: 16 (over y, z_hi), tensor: 2 (over z_lo).
Axes of the slice: x: 4, y: 4, z: 8 (z_hi: 4, z_lo: 2; z = z_hi * 2 + z_lo), core: 2. Of those that a mesh axis runs over, the one named last changes fastest.
Arguments:
- tokens: bfloat16 [1024, 7168], P(('dp', 'expert'), 'tensor'), may hold values from -6 to 6
- upstream: bfloat16 [1024, 7168], P(('dp', 'expert'), 'tensor'), may hold values from -3 to 3
- probs: bfloat16 [1024, 8], P(('dp', 'expert')), may hold values from 0.049804688 to 0.59765625
- routing: int32 [1024, 8], P(('dp', 'expert')), may hold values from 0 to 15, all different within a row; in each aligned block of 8 rows (0 to 7, 8 to 15, ...) at most 5 rows name the same one
- row_rollout: int32 [1024], P(('dp', 'expert')), may hold values from 0 to 255
- group_ids: int32 [256], replicated, may hold values from 0 to 31
- rewards: int32 [256], replicated, may hold values from 0 to 1
- w_gate: bfloat16 [16, 7168, 2048], P('expert', None, ('dp', 'tensor')), may hold values from -0.0625 to 0.0625
- w_up: bfloat16 [16, 7168, 2048], P('expert', None, ('dp', 'tensor')), may hold values from -0.0625 to 0.0625
- w_down: bfloat16 [16, 2048, 7168], P('expert', ('dp', 'tensor')), may hold values from -0.125 to 0.125
Outputs:
- input_grad: bfloat16 [1024, 7168], P(('dp', 'expert'), 'tensor')
- route_grad: bfloat16 [1024, 8], P(('dp', 'expert'))
- grad_gate: bfloat16 [16, 7168, 2048], P('expert', None, ('dp', 'tensor'))
- grad_up: bfloat16 [16, 7168, 2048], P('expert', None, ('dp', 'tensor'))
- grad_down: bfloat16 [16, 2048, 7168], P('expert', ('dp', 'tensor'))
Inputs may be any that keep to these rules, and one draw needn't show every extreme that they name: `routing`: each row names 8 different experts. Within each aligned block of 8 rows (the tokens of one index pair of dp and expert) no expert is named by more than 5 rows, a bound that some block reaches.
All inputs are finite; a program needn't handle non-finite values.
Results may differ from a plain program's by a relative error of at most 0.025.
Values may be sent and summed in bfloat16 or wider, within the bound.
No kernel may reach another device: no remote copies, remote signals or barrier semaphores. Data moves between devices by JAX's collectives and lax.ppermute only.
A program may use at most 128 MiB of HBM per device.

v0:
```python
import jax
import jax.numpy as jnp
from jax import lax
from jax.sharding import PartitionSpec as P


def advantages(row_rollout, group_ids, rewards):
    same_group = (group_ids[:, None] == group_ids[None, :]).astype(jnp.float32)
    reward_values = rewards.astype(jnp.float32)
    group_total = jnp.dot(same_group, reward_values, precision=lax.Precision.HIGHEST)
    group_count = jnp.sum(same_group, axis=1)
    per_rollout = reward_values - group_total / group_count
    member = (
        row_rollout[:, None] == jnp.arange(per_rollout.shape[0], dtype=jnp.int32)[None, :]
    ).astype(jnp.float32)
    return jnp.dot(member, per_rollout, precision=lax.Precision.HIGHEST)


def selection(routing, probs, experts, capacity):
    route_hits = (
        routing[:, :, None] == jnp.arange(experts, dtype=jnp.int32)[None, None, :]
    ).astype(jnp.float32)
    occupied = jnp.sum(route_hits, axis=1)
    weight = jnp.einsum("rke,rk->re", route_hits, probs.astype(jnp.float32))
    before = jnp.cumsum(occupied, axis=0) - occupied
    slot_index = jnp.arange(capacity, dtype=jnp.float32)
    chosen = occupied.T[:, None, :] * (before.T[:, None, :] == slot_index[None, :, None]).astype(
        jnp.float32
    )
    return (route_hits, weight, chosen)


def shards(tokens, upstream, probs, routing, row_rollout, group_ids, rewards, w_gate, w_up, w_down):
    f32 = jnp.float32
    bf16 = jnp.bfloat16
    experts = lax.axis_size("expert")
    dp_size = lax.axis_size("dp")
    tensor_size = lax.axis_size("tensor")
    group_rows, features = tokens.shape
    routes_per_row = routing.shape[1]
    capacity = min(group_rows, 5 * group_rows * routes_per_row // (4 * experts))
    slots = experts * capacity
    advantage = advantages(row_rollout, group_ids, rewards)
    cotangent = (advantage[:, None] * upstream.astype(f32)).astype(bf16)
    route_hits, weight, chosen = selection(routing, probs, experts, capacity)
    chosen_half = chosen.astype(bf16)
    both = jnp.stack([tokens, cotangent])
    packed = jnp.einsum("ecr,arf->aecf", chosen_half, both, preferred_element_type=f32).astype(bf16)
    packed_prob = jnp.einsum("ecr,re->ec", chosen, weight).astype(bf16)
    prob_row = jnp.zeros((experts, 1, features), bf16).at[:, 0, :capacity].set(packed_prob)
    chunk = slots + 8
    all_rows = dp_size * chunk
    extra = jnp.zeros((chunk - slots, features), bf16)
    tok_pack = jnp.concatenate([packed[0], prob_row], axis=1)
    arrived_tok = lax.all_to_all(tok_pack, "expert", split_axis=0, concat_axis=0, tiled=True)
    extra_prob = extra.at[0, :slots].set(arrived_tok[:, capacity, :capacity].reshape(slots))
    tok_rows = jnp.concatenate([arrived_tok[:, :capacity].reshape(slots, features), extra_prob])
    tok_rows, cot_pack = lax.optimization_barrier((tok_rows, packed[1]))
    arrived_cot = lax.all_to_all(cot_pack, "expert", split_axis=0, concat_axis=0, tiled=True)
    cot_rows = jnp.concatenate([arrived_cot.reshape(slots, features), extra])
    g_tok = lax.all_gather(tok_rows, ("tensor", "dp"), axis=0, tiled=True)
    g_tok = g_tok.reshape(tensor_size, all_rows, features)
    g_cot = lax.all_gather(cot_rows, ("tensor", "dp"), axis=0, tiled=True)
    g_cot = g_cot.reshape(tensor_size, all_rows, features)
    slot_prob = g_tok[0].reshape(dp_size, chunk, features)[:, slots, :chunk].reshape(all_rows)
    wg = w_gate[0].reshape(tensor_size, features, -1)
    wu = w_up[0].reshape(tensor_size, features, -1)
    wd = w_down[0]
    hidden_width = wd.shape[0]
    wd = wd.reshape(hidden_width, tensor_size, features)
    w_in = jnp.concatenate([wg, wu], axis=2)
    gate_up = sum(
        (jnp.dot(g_tok[t], w_in[t], preferred_element_type=f32) for t in range(tensor_size))
    )
    gate = gate_up[:, :hidden_width]
    up_part = gate_up[:, hidden_width:]
    back_hidden = jnp.einsum("tsf,htf->sh", g_cot, wd, preferred_element_type=f32)
    sigmoid_gate = jax.nn.sigmoid(gate)
    active = gate * sigmoid_gate
    hidden = (active * up_part).astype(bf16)
    hidden_wide = lax.optimization_barrier(hidden).astype(f32)
    route_part = jnp.sum(hidden_wide * back_hidden, axis=-1)
    scale = slot_prob.astype(f32)[:, None]
    scaled = scale * back_hidden
    grad_g = (scaled * up_part * sigmoid_gate * (1.0 + gate * (1.0 - sigmoid_gate))).astype(bf16)
    grad_u = (scaled * active).astype(bf16)
    weighted = (scale * hidden_wide).astype(bf16)
    grad_down = jnp.concatenate(
        [
            jnp.dot(weighted.T, g_cot[t], preferred_element_type=f32).astype(bf16)
            for t in range(tensor_size)
        ],
        axis=1,
    )
    grad_gate = jnp.concatenate(
        [
            jnp.dot(g_tok[t].T, grad_g, preferred_element_type=f32).astype(bf16)
            for t in range(tensor_size)
        ],
        axis=0,
    )
    grad_up = jnp.concatenate(
        [
            jnp.dot(g_tok[t].T, grad_u, preferred_element_type=f32).astype(bf16)
            for t in range(tensor_size)
        ],
        axis=0,
    )
    route_hi = route_part.astype(bf16).reshape(dp_size, chunk)
    route_lo = (route_part.reshape(dp_size, chunk) - route_hi.astype(f32)).astype(bf16)
    carry = jnp.zeros((dp_size, chunk, hidden_width), bf16)
    carry = carry.at[:, slots, :chunk].set(route_hi).at[:, slots + 1, :chunk].set(route_lo)
    lhs = jnp.concatenate([grad_g, grad_u, carry.reshape(all_rows, hidden_width)], axis=1)
    eye = (
        lax.broadcasted_iota(jnp.int32, (features, hidden_width), 0)
        == lax.broadcasted_iota(jnp.int32, (features, hidden_width), 1)
    ).astype(bf16)
    w_out = jnp.concatenate([wg, wu, jnp.broadcast_to(eye, wg.shape)], axis=2)
    product = jnp.einsum("sk,tfk->tsf", lhs, w_out, preferred_element_type=f32).astype(bf16)
    product = product.reshape(tensor_size * all_rows, features)
    own_rows = lax.psum_scatter(product, ("tensor", "dp"), scatter_dimension=0, tiled=True)
    own_rows, grad_gate, grad_up, grad_down = lax.optimization_barrier(
        (own_rows, grad_gate, grad_up, grad_down)
    )
    own_route = (
        own_rows[slots, :slots].astype(f32) + own_rows[slots + 1, :slots].astype(f32)
    ).astype(bf16)
    partner = lax.ppermute(own_route, "tensor", [(i, i ^ 1) for i in range(tensor_size)])
    own_route = jnp.where(lax.axis_index("tensor") == 0, own_route, partner)
    route_row = (
        jnp.zeros((experts, 1, features), bf16)
        .at[:, 0, :capacity]
        .set(own_route.reshape(experts, capacity))
    )
    back_pack = jnp.concatenate(
        [own_rows[:slots].reshape(experts, capacity, features), route_row], axis=1
    )
    home = lax.all_to_all(back_pack, "expert", split_axis=0, concat_axis=0, tiled=True)
    input_grad = jnp.einsum(
        "ecr,ecf->rf", chosen_half, home[:, :capacity], preferred_element_type=f32
    ).astype(bf16)
    per_expert = jnp.einsum("ecr,ec->re", chosen, home[:, capacity, :capacity].astype(f32))
    route_grad = jnp.einsum("rke,re->rk", route_hits, per_expert).astype(bf16)
    return (input_grad, route_grad, grad_gate[None], grad_up[None], grad_down[None])


def solution(mesh):
    in_specs = (
        P(("dp", "expert"), "tensor"),
        P(("dp", "expert"), "tensor"),
        P(("dp", "expert"), None),
        P(("dp", "expert"), None),
        P(("dp", "expert")),
        P(),
        P(),
        P("expert", None, ("dp", "tensor")),
        P("expert", None, ("dp", "tensor")),
        P("expert", ("dp", "tensor"), None),
    )
    out_specs = (
        P(("dp", "expert"), "tensor"),
        P(("dp", "expert"), None),
        P("expert", None, ("dp", "tensor")),
        P("expert", None, ("dp", "tensor")),
        P("expert", ("dp", "tensor"), None),
    )
    return jax.shard_map(shards, mesh=mesh, in_specs=in_specs, out_specs=out_specs, check_vma=False)
```

profile of v0, /device:TPU:7, one launch (start us, length us, event | category | flops | bytes accessed | tf_op | source)
XLA Modules:
  0.0 338.9 jit_solution(15449962634105801400)
XLA Ops:
  7.2 0.8 convert_reduce_fusion
  8.7 0.9 fusion.55
  9.7 1.0 fusion.53
  11.4 0.8 convolution_bitcast_fusion.1
  12.3 0.9 fusion.62
  13.2 1.3 fusion.15
  15.4 35.8 %all_to_all.15 = bf16[16,6,3584]{2,1,0:T(8,128)(2,1)S(1)} all-to-all(bf16[16,6,3584]{2,1,0:T(8,128)(2,1)S(1)} %copy.32), channel_id=1, replica_groups=mesh['dp'=8,'expert'=16,'tensor'=2] {'expert'}, dimensions={0} | all-to-all | bytes 1376256 | tf_op jit(solution)/shard_map/all_to_all | solution.py:55
  51.5 0.9 fusion.44
  52.8 37.7 %all_to_all.16 = bf16[16,5,3584]{2,1,0:T(8,128)(2,1)S(1)} all-to-all(bf16[16,5,3584]{2,1,0:T(8,128)(2,1)S(1)} %copy.33), channel_id=1, replica_groups=mesh['dp'=8,'expert'=16,'tensor'=2] {'expert'}, dimensions={0} | all-to-all | bytes 1146880 | tf_op jit(solution)/shard_map/all_to_all | solution.py:59
  90.7 0.9 concatenate.45
  92.2 2.3 reshape_squeeze.17
  94.6 33.8 %all-gather.3.cloned.1.call-done = bf16[1408,3584]{1,0:T(8,128)(2,1)} async-done(((bf16[88,3584]{1,0:T(8,128)(2,1)}), bf16[1408,3584]{1,0:T(8,128)(2,1)}) %all-gather.3.cloned.1.call-update) | async-done | bytes 10092560 | tf_op jit(solution)/shard_map/all_gather | solution.py:61
  128.4 2.4 slice-done.3
  130.9 4.3 %fusion.23 = f32[704,256]{1,0:T(8,128)S(1)} fusion(bf16[2,3584,128]{2,1,0:T(8,128)(2,1)} %bitcast.117, bf16[2,3584,128]{2,1,0:T(8,128)(2,1)S(1)} %bitcast.115, bf16[1408,3584]{1,0:T(8,128)(2,1)} %all-gather.3.cloned.1.call-done), kind=kOutput, calls=%fused_computation.28 | convolution fusion | flops 1295515648 | bytes 9437184 | tf_op jit(solution)/shard_map/dot_general | solution.py:73
  135.3 1.3 copy-done.2
  137.6 2.3 fusion.33
  139.9 53.8 %all-gather.5.cloned.1.call-done = bf16[1408,3584]{1,0:T(8,128)(2,1)} async-done(((bf16[88,3584]{1,0:T(8,128)(2,1)}), bf16[1408,3584]{1,0:T(8,128)(2,1)}) %all-gather.5.cloned.1.call-update) | async-done | bytes 10092560 | tf_op jit(solution)/shard_map/all_gather | solution.py:63
  193.7 6.8 %multiply_convert_fusion.2 = (bf16[704,128]{1,0:T(8,128)(2,1)S(1)}, bf16[704,128]{1,0:T(8,128)(2,1)S(1)}, bf16[704,128]{1,0:T(8,128)(2,1)S(1)}, f32[704,128]{1,0:T(8,128)S(1)}) fusion(f32[704,256]{1,0:T(8,128)} %fusion.33, f32[704]{0:T(1024)S(1)} %reshape.266, bf16[2,704,3584]{2,1,0:T(8,128)(2,1)} %bitcast.92, bf16[128,2,3584]{2,1,0:T(2,128)(2,1)S(1)} %copy-done.4), kind=kOutput, calls=%fused_computation.65 | convolution fusion | flops 1293287424 | bytes 13552384 | tf_op jit(solution)/shard_map/tsf,htf->sh/dot_general | solution.py:77
  201.2 9.4 %convolution_convert_fusion = bf16[2,3584,704]{1,2,0:T(8,128)(2,1)} fusion(bf16[2,3584,128]{2,1,0:T(8,128)(2,1)S(1)} %broadcast_in_dim.8, bf16[2,3584,128]{2,1,0:T(8,128)(2,1)} %bitcast.114, bf16[2,3584,128]{2,1,0:T(8,128)(2,1)} %bitcast.118, bf16[704,128]{1,0:T(8,128)(2,1)S(1)} %bitcast.101, bf16[704,128]{1,0:T(8,128)(2,1)S(1)} %get-tuple-element.80, ...), kind=kOutput, calls=%fused_computation | convolution fusion | flops 3898720256 | bytes 16138240 | tf_op jit(solution)/shard_map/sk,tfk->tsf/dot_general | solution.py:119
  210.7 3.4 %fusion.9 = bf16[128,3584]{1,0:T(8,128)(2,1)S(1)} fusion(bf16[1408,3584]{1,0:T(8,128)(2,1)} %all-gather.5.cloned.1.call-done, bf16[704,128]{1,0:T(8,128)(2,1)S(1)} %get-tuple-element.81, f32[704]{0:T(1024)S(1)} %reshape.266), kind=kOutput, calls=%fused_computation.11 | convolution fusion | flops 646651904 | bytes 6146816 | tf_op jit(solution)/shard_map/dot_general | solution.py:90
  214.1 3.6 %fusion.12 = bf16[128,3584]{1,0:T(8,128)(2,1)S(1)} fusion(bf16[1408,3584]{1,0:T(8,128)(2,1)} %all-gather.5.cloned.1.call-done, bf16[704,128]{1,0:T(8,128)(2,1)S(1)} %get-tuple-element.81, f32[704]{0:T(1024)S(1)} %reshape.266), kind=kOutput, calls=%fused_computation.12 | convolution fusion | flops 646651904 | bytes 6146816 | tf_op jit(solution)/shard_map/dot_general | solution.py:90
  217.7 4.5 %convolution_convert_fusion.2 = bf16[3584,128]{1,0:T(8,128)(2,1)S(1)} fusion(bf16[704,128]{1,0:T(8,128)(2,1)S(1)} %get-tuple-element.80, bf16[1408,3584]{1,0:T(8,128)(2,1)} %all-gather.3.cloned.1.call-done), kind=kOutput, calls=%fused_computation.13 | convolution fusion | flops 646381568 | bytes 6144000 | tf_op jit(solution)/shard_map/dot_general | solution.py:104
  222.3 1.7 convolution_convert_fusion.3
  224.0 1.7 convolution_convert_fusion.4
  225.7 1.7 convolution_convert_fusion.5
  227.4 1.4 pad_maximum_fusion.3
  228.8 2.1 pad_maximum_fusion.1
  230.9 59.5 %reduce-scatter.2.cloned.1.call-done = bf16[88,3584]{1,0:T(8,128)(2,1)} async-done(((bf16[1408,3584]{1,0:T(8,128)(2,1)}), bf16[88,3584]{1,0:T(8,128)(2,1)}) %reduce-scatter.2.cloned.1.call-update) | async-done | bytes 630800 | tf_op jit(solution)/shard_map/reduce_scatter | solution.py:121
  291.1 0.9 collective-permute-start
  292.0 1.1 slice.189
  294.6 35.8 %all_to_all.17 = bf16[16,6,3584]{2,1,0:T(8,128)(2,1)S(1)} all-to-all(bf16[16,6,3584]{2,1,0:T(8,128)(2,1)S(1)} %fusion.42), channel_id=1, replica_groups=mesh['dp'=8,'expert'=16,'tensor'=2] {'expert'}, dimensions={0} | all-to-all | bytes 1376256 | tf_op jit(solution)/shard_map/all_to_all | solution.py:138
  330.3 0.9 fusion.16
  (69 shorter events, 9.1 us)
Async XLA Ops:
  7.2 7.4 %copy-start = (bf16[8,8]{1,0:T(8,128)(2,1)S(1)}, bf16[8,8]{1,0:T(8,128)(2,1)}, u32[]{:S(2)}) copy-start(bf16[8,8]{1,0:T(8,128)(2,1)} %param.22) | copy-start | bytes 388
  7.2 121.2 %all-gather.3.cloned.1.call-start = ((), (), s32[]{:S(2)}) async-start(), calls=%async_computation.4 | async-start | bytes 10723328 | tf_op jit(solution)/shard_map/all_gather | solution.py:61
  12.3 2.3 copy-start.5
  52.4 141.3 %all-gather.5.cloned.1.call-start = ((), (), s32[]{:S(2)}) async-start(), calls=%async_computation.5 | async-start | bytes 10723328 | tf_op jit(solution)/shard_map/all_gather | solution.py:63
  90.5 1.7 copy-start.3
  91.6 198.7 %reduce-scatter.2.cloned.1.call-start = ((), (), s32[]{:S(2)}) async-start(), calls=%async_computation.6 | async-start | bytes 10723328 | tf_op jit(solution)/shard_map/reduce_scatter | solution.py:121
  94.6 36.4 %copy-start.6 = (bf16[1,7168,128]{2,1,0:T(8,128)(2,1)S(1)}, bf16[1,7168,128]{2,1,0:T(8,128)(2,1)}, u32[]{:S(2)}) copy-start(bf16[1,7168,128]{2,1,0:T(8,128)(2,1)} %param.28) | copy-start | bytes 5505028
  128.4 2.4 slice-start.3
  130.9 5.6 %copy-start.2 = (bf16[1408,3584]{1,0:T(8,128)(2,1)S(1)}, bf16[1408,3584]{1,0:T(8,128)(2,1)}, u32[]{:S(2)}) copy-start(bf16[1408,3584]{1,0:T(8,128)(2,1)} %all-gather.3.cloned.1.call-done) | copy-start | bytes 30277636
  130.9 6.1 %copy-start.7 = (bf16[1,7168,128]{2,1,0:T(8,128)(2,1)S(1)}, bf16[1,7168,128]{2,1,0:T(8,128)(2,1)}, u32[]{:S(2)}) copy-start(bf16[1,7168,128]{2,1,0:T(8,128)(2,1)} %param.28) | copy-start | bytes 5505028
  130.9 6.6 %copy-start.8 = (bf16[1,7168,128]{2,1,0:T(8,128)(2,1)S(1)}, bf16[1,7168,128]{2,1,0:T(8,128)(2,1)}, u32[]{:S(2)}) copy-start(bf16[1,7168,128]{2,1,0:T(8,128)(2,1)} %param.27) | copy-start | bytes 5505028
  137.6 56.2 %copy-start.4 = (bf16[128,2,3584]{2,1,0:T(2,128)(2,1)S(1)}, bf16[128,2,3584]{2,1,0:T(2,128)(2,1)}, u32[]{:S(2)}) copy-start(bf16[128,2,3584]{2,1,0:T(2,128)(2,1)} %reshape_squeeze.17) | copy-start | bytes 5505028
  214.1 8.1 %slice-start = ((s8[10092544]{0:T(1024)(128)(4,1)}), s8[4194304]{0:T(1024)(128)(4,1)S(1)}, s32[]{:S(2)}) async-start(s8[10092544]{0:T(1024)(128)(4,1)} %bitcast.93), calls=%async_computation.7 | async-start | bytes 8388608
  214.1 8.1 %slice-start.1 = ((s8[10092544]{0:T(1024)(128)(4,1)}), s8[4194304]{0:T(1024)(128)(4,1)S(1)}, s32[]{:S(2)}) async-start(s8[10092544]{0:T(1024)(128)(4,1)} %bitcast.93), calls=%async_computation.8 | async-start | bytes 8388608
  217.7 4.5 %slice-start.2 = ((s8[10092544]{0:T(1024)(128)(4,1)}), s8[1703936]{0:T(1024)(128)(4,1)S(1)}, s32[]{:S(2)}) async-start(s8[10092544]{0:T(1024)(128)(4,1)} %bitcast.93), calls=%async_computation.9 | async-start | bytes 3407872
  291.1 2.4 collective-permute-start
  294.2 38.1 %copy-start.1 = (bf16[8,8]{1,0:T(8,128)(2,1)S(1)}, bf16[8,8]{1,0:T(8,128)(2,1)}, u32[]{:S(2)}) copy-start(bf16[8,8]{1,0:T(8,128)(2,1)} %param.22) | copy-start | bytes 388
Sparse Core Ops, SparseCore 0:
  52.6 75.7 all-gather.2
  130.8 62.8 all-gather.4
  210.8 79.4 reduce-scatter.1
where the time goes:
time: 340 us; the launch traced here: 339 us
  waiting for transfers between devices  147 us (43%)
  blocking collectives  109 us (32%)
  matrix products  43.9 us (13%)
  between operations  14.1 us (4%)
  local copies, waits for them, and re-layouts  12.2 us (4%)
  other arithmetic  11.1 us (3%)
    reduce_scatter x1, waiting for transfers between devices, shards(): lax.psum_scatter(product, ('tensor', 'dp'), scatter_dimension=0, tiled=True)  59.5 us
    all_gather x1, waiting for transfers between devices, shards(): g_cot = lax.all_gather(cot_rows, ('tensor', 'dp'), axis=0, tiled=True)  53.8 us
    all_to_all x1, blocking collectives, shards(): lax.all_to_all(cot_pack, 'expert', split_axis=0, concat_axis=0, tiled=True)  37.7 us
    all_to_all x1, blocking collectives, shards(): lax.all_to_all(tok_pack, 'expert', split_axis=0, concat_axis=0, tiled=True)  35.8 us
    all_to_all x1, blocking collectives, shards(): lax.all_to_all(back_pack, 'expert', split_axis=0, concat_axis=0, tiled=True)  35.8 us
    all_gather x1, waiting for transfers between devices, shards(): g_tok = lax.all_gather(tok_rows, ('tensor', 'dp'), axis=0, tiled=True)  33.8 us
    dot_general x1, matrix products, shards(): jnp.einsum('sk,tfk->tsf', lhs, w_out, preferred_element_type=f32)  9.44 us
    dot_general x2, matrix products, shards(): jnp.dot(weighted.T, g_cot[t], preferred_element_type=f32).astype(bf16)  7 us
  transfers between devices with their start and end apart: 4, of which 4 were waited for; matrix products, arithmetic and copies ran while one was open for 9% of the time, Pallas kernels for 0%

commit v1 on v0

--- a/solution.py
+++ b/solution.py
@@ -60,7 +60,10 @@
     cot_rows = jnp.concatenate([arrived_cot.reshape(slots, features), extra])
     g_tok = lax.all_gather(tok_rows, ("tensor", "dp"), axis=0, tiled=True)
     g_tok = g_tok.reshape(tensor_size, all_rows, features)
-    g_cot = lax.all_gather(cot_rows, ("tensor", "dp"), axis=0, tiled=True)
+    size = lax.axis_size(("tensor", "dp"))
+    tiles = jnp.stack([cot_rows for _ in range(size)])
+    tiles = lax.all_to_all(tiles, ("tensor", "dp"), split_axis=0, concat_axis=0)
+    g_cot = jnp.concatenate(tiles, axis=0)
     g_cot = g_cot.reshape(tensor_size, all_rows, features)
     slot_prob = g_tok[0].reshape(dp_size, chunk, features)[:, slots, :chunk].reshape(all_rows)
     wg = w_gate[0].reshape(tensor_size, features, -1)

time: 340 us -> 403 us (1.19)
  waiting for transfers between devices: 147 us -> 193 us
  local copies, waits for them, and re-layouts: 12.2 us -> 22.3 us
  starting transfers between devices: 1.02 us -> 11 us
    all_gather x1, waiting for transfers between devices: 33.8 us -> 91.9 us  [shards(): g_tok = lax.all_gather(tok_rows, ('tensor', 'dp'), axis=0, tiled=True)]
    all_gather x1 -> x0, waiting for transfers between devices: 53.8 us -> none  [shards(): g_cot = lax.all_gather(cot_rows, ('tensor', 'dp'), axis=0, tiled=True)]
    all_to_all x0 -> x1, waiting for transfers between devices: none -> 42.1 us  [shards(): tiles = lax.all_to_all(tiles, ('tensor', 'dp'), split_axis=0, concat_axis=0)]
    all_to_all x0 -> x1, starting transfers between devices: none -> 9.7 us  [shards(): tiles = lax.all_to_all(tiles, ('tensor', 'dp'), split_axis=0, concat_axis=0)]
    slice x0 -> x1, local copies, waits for them, and re-layouts: none -> 6.92 us  [shards(): g_cot[t]]
    another operation x3 -> x4, local copies, waits for them, and re-layouts: 0.28 us -> 4.75 us  [the longest x1 4.46 us: shards(): tiles = jnp.stack([cot_rows for _ in range(size)])]
  transfers between devices with their start and end apart: 4 -> 4, of which waited for: 4 -> 3; matrix products, arithmetic and copies ran while one was open for 9% -> 10% of each run, Pallas kernels for 0% -> 0%
where the time goes in v1:
time: 403 us; the launch traced here: 402 us
  waiting for transfers between devices  193 us (48%)
  blocking collectives  109 us (27%)
  matrix products  41.5 us (10%)
  local copies, waits for them, and re-layouts  22.3 us (6%)
  between operations  14.4 us (4%)
  other arithmetic  11.2 us (3%)
  starting transfers between devices  11 us (3%)
    all_gather x1, waiting for transfers between devices, shards(): g_tok = lax.all_gather(tok_rows, ('tensor', 'dp'), axis=0, tiled=True)  91.9 us
    reduce_scatter x1, waiting for transfers between devices, shards(): lax.psum_scatter(product, ('tensor', 'dp'), scatter_dimension=0, tiled=True)  58.7 us
    all_to_all x1, waiting for transfers between devices, shards(): tiles = lax.all_to_all(tiles, ('tensor', 'dp'), split_axis=0, concat_axis=0)  42.1 us
    all_to_all x1, blocking collectives, shards(): lax.all_to_all(cot_pack, 'expert', split_axis=0, concat_axis=0, tiled=True)  37.8 us
    all_to_all x1, blocking collectives, shards(): lax.all_to_all(back_pack, 'expert', split_axis=0, concat_axis=0, tiled=True)  35.7 us
    all_to_all x1, blocking collectives, shards(): lax.all_to_all(tok_pack, 'expert', split_axis=0, concat_axis=0, tiled=True)  35.6 us
    all_to_all x1, starting transfers between devices, shards(): tiles = lax.all_to_all(tiles, ('tensor', 'dp'), split_axis=0, concat_axis=0)  9.7 us
    dot_general x1, matrix products, shards(): jnp.einsum('sk,tfk->tsf', lhs, w_out, preferred_element_type=f32)  9.44 us
  transfers between devices with their start and end apart: 4, of which 3 were waited for; matrix products, arithmetic and copies ran while one was open for 10% of the time, Pallas kernels for 0%

profile of v1, /device:TPU:7, one launch (start us, length us, event | category | flops | bytes accessed | tf_op | source)
XLA Modules:
  0.0 402.2 jit_solution(14571382855347355605)
XLA Ops:
  8.7 0.9 fusion.45
  9.7 1.0 fusion.43
  12.3 0.9 fusion.52
  13.2 1.3 fusion.5
  15.4 35.6 %all_to_all.20 = bf16[16,6,3584]{2,1,0:T(8,128)(2,1)S(1)} all-to-all(bf16[16,6,3584]{2,1,0:T(8,128)(2,1)S(1)} %copy.32), channel_id=1, replica_groups=mesh['dp'=8,'expert'=16,'tensor'=2] {'expert'}, dimensions={0} | all-to-all | bytes 1376256 | tf_op jit(solution)/shard_map/all_to_all | solution.py:55
  51.4 0.9 fusion.34
  52.7 37.8 %all_to_all.21 = bf16[16,5,3584]{2,1,0:T(8,128)(2,1)S(1)} all-to-all(bf16[16,5,3584]{2,1,0:T(8,128)(2,1)S(1)} %copy.33), channel_id=1, replica_groups=mesh['dp'=8,'expert'=16,'tensor'=2] {'expert'}, dimensions={0} | all-to-all | bytes 1146880 | tf_op jit(solution)/shard_map/all_to_all | solution.py:59
  90.7 4.5 %stack.11 = bf16[16,88,3584]{2,1,0:T(8,128)(2,1)} broadcast(bf16[88,3584]{1,0:T(8,128)(2,1)S(1)} %concatenate.45), dimensions={1,2} | broadcast | bytes 10723328 | tf_op jit(solution)/shard_map/stack | solution.py:64
  95.2 9.7 %all-to-all-start.2 = ((bf16[16,88,3584]{2,1,0:T(8,128)(2,1)}), bf16[16,88,3584]{2,1,0:T(8,128)(2,1)}, u32[]{:S(2)}, u32[]{:S(2)}) async-start(bf16[16,88,3584]{2,1,0:T(8,128)(2,1)} %stack.11), calls=%async_computation.2 | async-start | bytes 20185088 | tf_op jit(solution)/shard_map/all_to_all | solution.py:65
  104.9 2.3 reshape_squeeze.17
  107.3 91.9 %all-gather.2.cloned.1.call-done = bf16[1408,3584]{1,0:T(8,128)(2,1)} async-done(((bf16[88,3584]{1,0:T(8,128)(2,1)}), bf16[1408,3584]{1,0:T(8,128)(2,1)}) %all-gather.2.cloned.1.call-update) | async-done | bytes 10092560 | tf_op jit(solution)/shard_map/all_gather | solution.py:61
  199.2 2.4 slice-done.3
  201.8 4.3 %fusion.13 = f32[704,256]{1,0:T(8,128)S(1)} fusion(bf16[2,3584,128]{2,1,0:T(8,128)(2,1)} %bitcast.122, bf16[2,3584,128]{2,1,0:T(8,128)(2,1)S(1)} %bitcast.120, bf16[1408,3584]{1,0:T(8,128)(2,1)} %all-gather.2.cloned.1.call-done), kind=kOutput, calls=%fused_computation.24 | convolution fusion | flops 1295515648 | bytes 9437184 | tf_op jit(solution)/shard_map/dot_general | solution.py:76
  206.1 1.3 copy-done.2
  208.4 2.3 fusion.23
  210.7 42.1 %all-to-all-done.2 = bf16[16,88,3584]{2,1,0:T(8,128)(2,1)} async-done(((bf16[16,88,3584]{2,1,0:T(8,128)(2,1)}), bf16[16,88,3584]{2,1,0:T(8,128)(2,1)}, u32[]{:S(2)}, u32[]{:S(2)}) %all-to-all-start.2) | async-done | bytes 10092576 | tf_op jit(solution)/shard_map/all_to_all | solution.py:65
  252.9 6.8 %multiply_convert_fusion.2 = (bf16[704,128]{1,0:T(8,128)(2,1)S(1)}, bf16[704,128]{1,0:T(8,128)(2,1)S(1)}, bf16[704,128]{1,0:T(8,128)(2,1)S(1)}, f32[704,128]{1,0:T(8,128)S(1)}) fusion(f32[704,256]{1,0:T(8,128)} %fusion.23, f32[704]{0:T(1024)S(1)} %reshape.264, bf16[2,704,3584]{2,1,0:T(8,128)(2,1)} %bitcast.24, bf16[128,2,3584]{2,1,0:T(2,128)(2,1)S(1)} %copy-done.4), kind=kOutput, calls=%fused_computation.61 | convolution fusion | flops 1293287424 | bytes 13552384 | tf_op jit(solution)/shard_map/tsf,htf->sh/dot_general | solution.py:80
  260.4 9.4 %convolution_convert_fusion = bf16[2,3584,704]{1,2,0:T(8,128)(2,1)} fusion(bf16[2,3584,128]{2,1,0:T(8,128)(2,1)S(1)} %broadcast_in_dim.8, bf16[2,3584,128]{2,1,0:T(8,128)(2,1)} %bitcast.119, bf16[2,3584,128]{2,1,0:T(8,128)(2,1)} %bitcast.123, bf16[704,128]{1,0:T(8,128)(2,1)S(1)} %bitcast.106, bf16[704,128]{1,0:T(8,128)(2,1)S(1)} %get-tuple-element.82, ...), kind=kOutput, calls=%fused_computation | convolution fusion | flops 3898720256 | bytes 16138240 | tf_op jit(solution)/shard_map/sk,tfk->tsf/dot_general | solution.py:122
  269.8 6.9 %fusion.80 = (bf16[8,88,3584]{2,1,0:T(8,128)(2,1)}, bf16[8,88,3584]{2,1,0:T(8,128)(2,1)S(1)}) fusion(bf16[16,88,3584]{2,1,0:T(8,128)(2,1)} %all-to-all-done.2), kind=kLoop, calls=%fused_computation.117 | loop fusion | bytes 20185088 | tf_op jit(solution)/shard_map/slice | solution.py:93
  276.8 3.4 convolution_convert_fusion.3
  280.2 1.0 convolution_convert_fusion.2
  281.2 4.6 %convolution_convert_fusion.4 = bf16[3584,128]{1,0:T(8,128)(2,1)S(1)} fusion(bf16[704,128]{1,0:T(8,128)(2,1)S(1)} %get-tuple-element.82, bf16[1408,3584]{1,0:T(8,128)(2,1)} %all-gather.2.cloned.1.call-done), kind=kOutput, calls=%fused_computation.9 | convolution fusion | flops 646381568 | bytes 6144000 | tf_op jit(solution)/shard_map/dot_general | solution.py:107
  285.9 1.7 convolution_convert_fusion.5
  287.6 1.7 convolution_convert_fusion.6
  289.3 1.7 convolution_convert_fusion.7
  291.0 1.4 pad_maximum_fusion.3
  292.4 2.1 pad_maximum_fusion.1
  294.5 58.7 %reduce-scatter.2.cloned.1.call-done = bf16[88,3584]{1,0:T(8,128)(2,1)} async-done(((bf16[1408,3584]{1,0:T(8,128)(2,1)}), bf16[88,3584]{1,0:T(8,128)(2,1)}) %reduce-scatter.2.cloned.1.call-update) | async-done | bytes 630800 | tf_op jit(solution)/shard_map/reduce_scatter | solution.py:124
  353.9 1.2 collective-permute-start
  355.1 1.1 slice.189
  357.6 35.7 %all_to_all.22 = bf16[16,6,3584]{2,1,0:T(8,128)(2,1)S(1)} all-to-all(bf16[16,6,3584]{2,1,0:T(8,128)(2,1)S(1)} %fusion.32), channel_id=1, replica_groups=mesh['dp'=8,'expert'=16,'tensor'=2] {'expert'}, dimensions={0} | all-to-all | bytes 1376256 | tf_op jit(solution)/shard_map/all_to_all | solution.py:141
  393.3 0.9 fusion.6
  (70 shorter events, 10.1 us)
Async XLA Ops:
  7.2 7.4 %copy-start = (bf16[8,8]{1,0:T(8,128)(2,1)S(1)}, bf16[8,8]{1,0:T(8,128)(2,1)}, u32[]{:S(2)}) copy-start(bf16[8,8]{1,0:T(8,128)(2,1)} %param.22) | copy-start | bytes 388
  7.2 7.4 %copy-start.5 = (s32[8,8]{1,0:T(8,128)S(1)}, s32[8,8]{1,0:T(8,128)}, u32[]{:S(2)}) copy-start(s32[8,8]{1,0:T(8,128)} %param.23) | copy-start | bytes 772
  7.2 192.0 %all-gather.2.cloned.1.call-start = ((), (), s32[]{:S(2)}) async-start(), calls=%async_computation.5 | async-start | bytes 10723328 | tf_op jit(solution)/shard_map/all_gather | solution.py:61
  95.2 9.7 %copy-start.3 = (bf16[1,128,7168]{2,1,0:T(8,128)(2,1)S(1)}, bf16[1,128,7168]{2,1,0:T(8,128)(2,1)}, u32[]{:S(2)}) copy-start(bf16[1,128,7168]{2,1,0:T(8,128)(2,1)} %param.29) | copy-start | bytes 5505028
  95.2 157.7 %all-to-all-start.2 = ((bf16[16,88,3584]{2,1,0:T(8,128)(2,1)}), bf16[16,88,3584]{2,1,0:T(8,128)(2,1)}, u32[]{:S(2)}, u32[]{:S(2)}) async-start(bf16[16,88,3584]{2,1,0:T(8,128)(2,1)} %stack.11), calls=%async_computation.2 | async-start | bytes 20185088 | tf_op jit(solution)/shard_map/all_to_all | solution.py:65
  104.9 248.3 %reduce-scatter.2.cloned.1.call-start = ((), (), s32[]{:S(2)}) async-start(), calls=%async_computation.6 | async-start | bytes 10723328 | tf_op jit(solution)/shard_map/reduce_scatter | solution.py:124
  107.3 94.5 %copy-start.6 = (bf16[1,7168,128]{2,1,0:T(8,128)(2,1)S(1)}, bf16[1,7168,128]{2,1,0:T(8,128)(2,1)}, u32[]{:S(2)}) copy-start(bf16[1,7168,128]{2,1,0:T(8,128)(2,1)} %param.28) | copy-start | bytes 5505028
  199.2 2.4 slice-start.3
  201.7 5.6 %copy-start.2 = (bf16[1408,3584]{1,0:T(8,128)(2,1)S(1)}, bf16[1408,3584]{1,0:T(8,128)(2,1)}, u32[]{:S(2)}) copy-start(bf16[1408,3584]{1,0:T(8,128)(2,1)} %all-gather.2.cloned.1.call-done) | copy-start | bytes 30277636
  201.8 6.1 %copy-start.7 = (bf16[1,7168,128]{2,1,0:T(8,128)(2,1)S(1)}, bf16[1,7168,128]{2,1,0:T(8,128)(2,1)}, u32[]{:S(2)}) copy-start(bf16[1,7168,128]{2,1,0:T(8,128)(2,1)} %param.28) | copy-start | bytes 5505028
  201.8 6.6 %copy-start.8 = (bf16[1,7168,128]{2,1,0:T(8,128)(2,1)S(1)}, bf16[1,7168,128]{2,1,0:T(8,128)(2,1)}, u32[]{:S(2)}) copy-start(bf16[1,7168,128]{2,1,0:T(8,128)(2,1)} %param.27) | copy-start | bytes 5505028
  208.4 44.5 %copy-start.4 = (bf16[128,2,3584]{2,1,0:T(2,128)(2,1)S(1)}, bf16[128,2,3584]{2,1,0:T(2,128)(2,1)}, u32[]{:S(2)}) copy-start(bf16[128,2,3584]{2,1,0:T(2,128)(2,1)} %reshape_squeeze.17) | copy-start | bytes 5505028
  280.2 5.6 %slice-start = ((s8[10092544]{0:T(1024)(128)(4,1)}), s8[4194304]{0:T(1024)(128)(4,1)S(1)}, s32[]{:S(2)}) async-start(s8[10092544]{0:T(1024)(128)(4,1)} %bitcast.98), calls=%async_computation.7 | async-start | bytes 8388608
  280.2 5.6 %slice-start.1 = ((s8[10092544]{0:T(1024)(128)(4,1)}), s8[4194304]{0:T(1024)(128)(4,1)S(1)}, s32[]{:S(2)}) async-start(s8[10092544]{0:T(1024)(128)(4,1)} %bitcast.98), calls=%async_computation.8 | async-start | bytes 8388608
  281.2 4.6 %slice-start.2 = ((s8[10092544]{0:T(1024)(128)(4,1)}), s8[1703936]{0:T(1024)(128)(4,1)S(1)}, s32[]{:S(2)}) async-start(s8[10092544]{0:T(1024)(128)(4,1)} %bitcast.98), calls=%async_computation.9 | async-start | bytes 3407872
  353.9 2.6 collective-permute-start
  356.2 39.1 %copy-start.1 = (bf16[8,8]{1,0:T(8,128)(2,1)S(1)}, bf16[8,8]{1,0:T(8,128)(2,1)}, u32[]{:S(2)}) copy-start(bf16[8,8]{1,0:T(8,128)(2,1)} %param.22) | copy-start | bytes 388
Sparse Core Ops, SparseCore 0:
  52.4 146.7 all-gather.1
  270.0 83.1 reduce-scatter.1
